TPU v7x, 512 devices: a whole 4x8x8 slice. The times are simulated.
512 devices in a mesh: sep: 8 (over y), row: 8 (over z), col: 8 (over x, core).
Axes of the slice: x: 4, y: 8, z: 8, core: 2. Of those that a mesh axis runs over, the one named last changes fastest.
Arguments:
- right_sides: float32 [2, 16, 32768], P(None, None, ('sep', 'row', 'col')), may hold values from -6 to 6
- inverse_diag: float32 [8, 4096, 4096], P('sep', ('row', 'col')), may hold values from -0.09375 to 0.09375
- lower_blocks: float32 [8, 2048, 4096], P('sep', ('row', 'col')), may hold values from -0.09375 to 0.09375
- targets: int32 [8, 2048], P('sep', ('row', 'col')), may hold values from 0 to 32767, as said below
- counts: int32 [8, 64], P('sep', ('row', 'col')), may hold values from 0 to 32, as said below
Outputs:
- solution: float32 [2, 16, 32768], P(None, None, ('sep', 'row', 'col'))
Inputs may be any that keep to these rules, and one draw needn't show every extreme that they name: For every separator s and lower row j: targets[s, j] // 4096 > s, except for the last separator whose counts are all zero; and (targets[s, j] % 4096) // 64 == j // 32. The last separator's counts are zero; every other separator has a block with exactly 32 live rows, and the others at least one.
All inputs are finite; a program needn't handle non-finite values.
Results may differ from a plain program's by a relative error of at most 0.0001.
Values sent between devices are 32-bit elements; how exact they have to be, the bound alone decides.
No kernel may reach another device: no remote copies, remote signals or barrier semaphores. Data moves between devices by JAX's collectives and lax.ppermute only.
A program may use at most 64 MiB of HBM per device.

v0:
```python
import jax
import jax.numpy as jnp
from jax import lax
from jax.sharding import PartitionSpec as P

W = 4096


def passed_along(block, axis, distance):
    devices = range(lax.axis_size(axis))
    route = [(i - distance, i) for i in devices if i - distance in devices]
    return lax.ppermute(block, axis, route)


def shards(right_sides, inverse_diag, lower_blocks, targets, counts):
    levels = lax.axis_size("sep")
    own_level = lax.axis_index("sep")
    batches = right_sides.shape[0]
    width_rhs = right_sides.shape[1]
    own_rows = right_sides.shape[2]
    diag_rows = inverse_diag[0]
    lower_rows = lower_blocks[0]
    lower_count = lower_rows.shape[0]
    live = jnp.arange(lower_count, dtype=jnp.int32) < counts[0, 0]
    places = targets[0] // W * own_rows + targets[0] % own_rows

    def solve_piece(segment):
        return lax.dot_general(
            segment,
            diag_rows,
            (((1,), (1,)), ((), ())),
            precision=lax.Precision.HIGHEST,
            preferred_element_type=jnp.float32,
        )

    def lower_piece(segment):
        return lax.dot_general(
            segment,
            lower_rows,
            (((1,), (1,)), ((), ())),
            precision=lax.Precision.HIGHEST,
            preferred_element_type=jnp.float32,
        )

    def one_turn(turn, state):
        carried, solved_all = state
        batch_now = turn // levels
        active = turn % levels == own_level
        batch_now = jnp.clip(batch_now, 0, batches - 1)
        given = lax.dynamic_index_in_dim(right_sides, batch_now, 0, keepdims=False)
        resid = given - lax.dynamic_slice_in_dim(carried, own_level * own_rows, own_rows, 1)
        solved = solve_piece(lax.all_gather(resid, ("row", "col"), axis=1, tiled=True))
        update = lower_piece(lax.all_gather(solved, ("row", "col"), axis=1, tiled=True))
        update = jnp.where(live[None, :], update, jnp.float32(0.0))
        carried = carried.at[:, places].add(update)
        former = lax.dynamic_index_in_dim(solved_all, batch_now, 0, keepdims=False)
        solved_all = lax.dynamic_update_index_in_dim(
            solved_all, jnp.where(active, solved, former), batch_now, 0
        )
        carried = passed_along(carried, "sep", 1)
        return (carried, solved_all)

    turns = batches * levels
    start_carry = jnp.zeros((width_rhs, levels * own_rows), jnp.float32)
    start_solved = jnp.zeros(right_sides.shape, jnp.float32)
    final_carry, solution = lax.fori_loop(0, turns, one_turn, (start_carry, start_solved))
    return solution


def solution(mesh):
    placed = (
        P(None, None, ("sep", "row", "col")),
        P("sep", ("row", "col"), None),
        P("sep", ("row", "col"), None),
        P("sep", ("row", "col")),
        P("sep", ("row", "col")),
    )
    return jax.shard_map(
        shards,
        mesh=mesh,
        in_specs=placed,
        out_specs=P(None, None, ("sep", "row", "col")),
        check_vma=False,
    )
```

profile of v0, /device:TPU:32, one launch (start us, length us, event | category | flops | bytes accessed | tf_op | source)
XLA Modules:
  0.0 1837.8 jit_solution(4809233854240847362)
XLA Ops:
  1.4 1835.8 %while.18 = (s32[]{:T(128)}, f32[16,512]{0,1:T(8,128)S(1)}, f32[2,16,64]{2,1,0:T(8,128)S(1)}, s32[32]{0:T(128)S(1)}, f32[2,16,64]{2,1,0:T(8,128)S(1)}, /*index=5...) while((s32[]{:T(128)}, f32[16,512]{0,1:T(8,128)S(1)}, ...), condition=%wide.region_2.3_spmd.clone, body=%wide.region_0.2_spmd.clone.sunk | while | flops 75500688 | bytes 11338590 | solution.py:66
  1.6 56.5 %all-gather.6 = f32[64,64,16]{1,2,0:T(8,128)S(1)} all-gather(f32[1,64,16]{1,2,0:T(8,128)S(1)} %fusion.22), channel_id=1, replica_groups=mesh['sep'=8,'row'=8,'col'=8] {'row','col'}, dimensions={0}, use_global_device_ids=true | all-gather | bytes 266240 | tf_op jit(solution)/shard_map/while/body/eval_jaxpr/all_gather | solution.py:52
  60.2 49.5 %all-gather.7 = f32[64,64,16]{1,2,0:T(8,128)S(1)} all-gather(f32[1,64,16]{1,2,0:T(8,128)S(1)} %bitcast.71), channel_id=1, replica_groups=mesh['sep'=8,'row'=8,'col'=8] {'row','col'}, dimensions={0}, use_global_device_ids=true | all-gather | bytes 266240 | tf_op jit(solution)/shard_map/while/body/eval_jaxpr/all_gather | solution.py:53
  112.5 2.6 collective-permute-start
  115.0 9.1 collective-permute-done
  124.3 48.0 %all-gather.6 = f32[64,64,16]{1,2,0:T(8,128)S(1)} all-gather(f32[1,64,16]{1,2,0:T(8,128)S(1)} %fusion.22), channel_id=1, replica_groups=mesh['sep'=8,'row'=8,'col'=8] {'row','col'}, dimensions={0}, use_global_device_ids=true | all-gather | bytes 266240 | tf_op jit(solution)/shard_map/while/body/eval_jaxpr/all_gather | solution.py:52
  174.4 49.5 %all-gather.7 = f32[64,64,16]{1,2,0:T(8,128)S(1)} all-gather(f32[1,64,16]{1,2,0:T(8,128)S(1)} %bitcast.71), channel_id=1, replica_groups=mesh['sep'=8,'row'=8,'col'=8] {'row','col'}, dimensions={0}, use_global_device_ids=true | all-gather | bytes 266240 | tf_op jit(solution)/shard_map/while/body/eval_jaxpr/all_gather | solution.py:53
  226.7 1.9 collective-permute-start
  228.6 9.7 collective-permute-done
  238.5 48.0 %all-gather.6 = f32[64,64,16]{1,2,0:T(8,128)S(1)} all-gather(f32[1,64,16]{1,2,0:T(8,128)S(1)} %fusion.22), channel_id=1, replica_groups=mesh['sep'=8,'row'=8,'col'=8] {'row','col'}, dimensions={0}, use_global_device_ids=true | all-gather | bytes 266240 | tf_op jit(solution)/shard_map/while/body/eval_jaxpr/all_gather | solution.py:52
  288.6 49.5 %all-gather.7 = f32[64,64,16]{1,2,0:T(8,128)S(1)} all-gather(f32[1,64,16]{1,2,0:T(8,128)S(1)} %bitcast.71), channel_id=1, replica_groups=mesh['sep'=8,'row'=8,'col'=8] {'row','col'}, dimensions={0}, use_global_device_ids=true | all-gather | bytes 266240 | tf_op jit(solution)/shard_map/while/body/eval_jaxpr/all_gather | solution.py:53
  340.9 1.9 collective-permute-start
  342.8 9.7 collective-permute-done
  352.7 48.0 %all-gather.6 = f32[64,64,16]{1,2,0:T(8,128)S(1)} all-gather(f32[1,64,16]{1,2,0:T(8,128)S(1)} %fusion.22), channel_id=1, replica_groups=mesh['sep'=8,'row'=8,'col'=8] {'row','col'}, dimensions={0}, use_global_device_ids=true | all-gather | bytes 266240 | tf_op jit(solution)/shard_map/while/body/eval_jaxpr/all_gather | solution.py:52
  402.8 49.5 %all-gather.7 = f32[64,64,16]{1,2,0:T(8,128)S(1)} all-gather(f32[1,64,16]{1,2,0:T(8,128)S(1)} %bitcast.71), channel_id=1, replica_groups=mesh['sep'=8,'row'=8,'col'=8] {'row','col'}, dimensions={0}, use_global_device_ids=true | all-gather | bytes 266240 | tf_op jit(solution)/shard_map/while/body/eval_jaxpr/all_gather | solution.py:53
  455.1 1.9 collective-permute-start
  457.0 9.7 collective-permute-done
  467.0 48.0 %all-gather.6 = f32[64,64,16]{1,2,0:T(8,128)S(1)} all-gather(f32[1,64,16]{1,2,0:T(8,128)S(1)} %fusion.22), channel_id=1, replica_groups=mesh['sep'=8,'row'=8,'col'=8] {'row','col'}, dimensions={0}, use_global_device_ids=true | all-gather | bytes 266240 | tf_op jit(solution)/shard_map/while/body/eval_jaxpr/all_gather | solution.py:52
  517.0 49.5 %all-gather.7 = f32[64,64,16]{1,2,0:T(8,128)S(1)} all-gather(f32[1,64,16]{1,2,0:T(8,128)S(1)} %bitcast.71), channel_id=1, replica_groups=mesh['sep'=8,'row'=8,'col'=8] {'row','col'}, dimensions={0}, use_global_device_ids=true | all-gather | bytes 266240 | tf_op jit(solution)/shard_map/while/body/eval_jaxpr/all_gather | solution.py:53
  569.3 1.9 collective-permute-start
  571.2 9.7 collective-permute-done
  581.2 48.0 %all-gather.6 = f32[64,64,16]{1,2,0:T(8,128)S(1)} all-gather(f32[1,64,16]{1,2,0:T(8,128)S(1)} %fusion.22), channel_id=1, replica_groups=mesh['sep'=8,'row'=8,'col'=8] {'row','col'}, dimensions={0}, use_global_device_ids=true | all-gather | bytes 266240 | tf_op jit(solution)/shard_map/while/body/eval_jaxpr/all_gather | solution.py:52
  631.3 49.5 %all-gather.7 = f32[64,64,16]{1,2,0:T(8,128)S(1)} all-gather(f32[1,64,16]{1,2,0:T(8,128)S(1)} %bitcast.71), channel_id=1, replica_groups=mesh['sep'=8,'row'=8,'col'=8] {'row','col'}, dimensions={0}, use_global_device_ids=true | all-gather | bytes 266240 | tf_op jit(solution)/shard_map/while/body/eval_jaxpr/all_gather | solution.py:53
  683.5 1.9 collective-permute-start
  685.4 9.7 collective-permute-done
  695.4 48.0 %all-gather.6 = f32[64,64,16]{1,2,0:T(8,128)S(1)} all-gather(f32[1,64,16]{1,2,0:T(8,128)S(1)} %fusion.22), channel_id=1, replica_groups=mesh['sep'=8,'row'=8,'col'=8] {'row','col'}, dimensions={0}, use_global_device_ids=true | all-gather | bytes 266240 | tf_op jit(solution)/shard_map/while/body/eval_jaxpr/all_gather | solution.py:52
  745.5 49.5 %all-gather.7 = f32[64,64,16]{1,2,0:T(8,128)S(1)} all-gather(f32[1,64,16]{1,2,0:T(8,128)S(1)} %bitcast.71), channel_id=1, replica_groups=mesh['sep'=8,'row'=8,'col'=8] {'row','col'}, dimensions={0}, use_global_device_ids=true | all-gather | bytes 266240 | tf_op jit(solution)/shard_map/while/body/eval_jaxpr/all_gather | solution.py:53
  797.7 1.9 collective-permute-start
  799.6 9.7 collective-permute-done
  809.6 48.0 %all-gather.6 = f32[64,64,16]{1,2,0:T(8,128)S(1)} all-gather(f32[1,64,16]{1,2,0:T(8,128)S(1)} %fusion.22), channel_id=1, replica_groups=mesh['sep'=8,'row'=8,'col'=8] {'row','col'}, dimensions={0}, use_global_device_ids=true | all-gather | bytes 266240 | tf_op jit(solution)/shard_map/while/body/eval_jaxpr/all_gather | solution.py:52
  859.7 49.5 %all-gather.7 = f32[64,64,16]{1,2,0:T(8,128)S(1)} all-gather(f32[1,64,16]{1,2,0:T(8,128)S(1)} %bitcast.71), channel_id=1, replica_groups=mesh['sep'=8,'row'=8,'col'=8] {'row','col'}, dimensions={0}, use_global_device_ids=true | all-gather | bytes 266240 | tf_op jit(solution)/shard_map/while/body/eval_jaxpr/all_gather | solution.py:53
  911.9 1.9 collective-permute-start
  913.8 9.7 collective-permute-done
  923.8 48.0 %all-gather.6 = f32[64,64,16]{1,2,0:T(8,128)S(1)} all-gather(f32[1,64,16]{1,2,0:T(8,128)S(1)} %fusion.22), channel_id=1, replica_groups=mesh['sep'=8,'row'=8,'col'=8] {'row','col'}, dimensions={0}, use_global_device_ids=true | all-gather | bytes 266240 | tf_op jit(solution)/shard_map/while/body/eval_jaxpr/all_gather | solution.py:52
  973.9 49.5 %all-gather.7 = f32[64,64,16]{1,2,0:T(8,128)S(1)} all-gather(f32[1,64,16]{1,2,0:T(8,128)S(1)} %bitcast.71), channel_id=1, replica_groups=mesh['sep'=8,'row'=8,'col'=8] {'row','col'}, dimensions={0}, use_global_device_ids=true | all-gather | bytes 266240 | tf_op jit(solution)/shard_map/while/body/eval_jaxpr/all_gather | solution.py:53
  1026.1 1.9 collective-permute-start
  1028.0 9.7 collective-permute-done
  1038.0 48.0 %all-gather.6 = f32[64,64,16]{1,2,0:T(8,128)S(1)} all-gather(f32[1,64,16]{1,2,0:T(8,128)S(1)} %fusion.22), channel_id=1, replica_groups=mesh['sep'=8,'row'=8,'col'=8] {'row','col'}, dimensions={0}, use_global_device_ids=true | all-gather | bytes 266240 | tf_op jit(solution)/shard_map/while/body/eval_jaxpr/all_gather | solution.py:52
  1088.1 49.5 %all-gather.7 = f32[64,64,16]{1,2,0:T(8,128)S(1)} all-gather(f32[1,64,16]{1,2,0:T(8,128)S(1)} %bitcast.71), channel_id=1, replica_groups=mesh['sep'=8,'row'=8,'col'=8] {'row','col'}, dimensions={0}, use_global_device_ids=true | all-gather | bytes 266240 | tf_op jit(solution)/shard_map/while/body/eval_jaxpr/all_gather | solution.py:53
  1140.3 1.9 collective-permute-start
  1142.2 9.7 collective-permute-done
  1152.2 48.0 %all-gather.6 = f32[64,64,16]{1,2,0:T(8,128)S(1)} all-gather(f32[1,64,16]{1,2,0:T(8,128)S(1)} %fusion.22), channel_id=1, replica_groups=mesh['sep'=8,'row'=8,'col'=8] {'row','col'}, dimensions={0}, use_global_device_ids=true | all-gather | bytes 266240 | tf_op jit(solution)/shard_map/while/body/eval_jaxpr/all_gather | solution.py:52
  1202.3 49.5 %all-gather.7 = f32[64,64,16]{1,2,0:T(8,128)S(1)} all-gather(f32[1,64,16]{1,2,0:T(8,128)S(1)} %bitcast.71), channel_id=1, replica_groups=mesh['sep'=8,'row'=8,'col'=8] {'row','col'}, dimensions={0}, use_global_device_ids=true | all-gather | bytes 266240 | tf_op jit(solution)/shard_map/while/body/eval_jaxpr/all_gather | solution.py:53
  1254.5 1.9 collective-permute-start
  1256.4 9.7 collective-permute-done
  1266.4 48.0 %all-gather.6 = f32[64,64,16]{1,2,0:T(8,128)S(1)} all-gather(f32[1,64,16]{1,2,0:T(8,128)S(1)} %fusion.22), channel_id=1, replica_groups=mesh['sep'=8,'row'=8,'col'=8] {'row','col'}, dimensions={0}, use_global_device_ids=true | all-gather | bytes 266240 | tf_op jit(solution)/shard_map/while/body/eval_jaxpr/all_gather | solution.py:52
  1316.5 49.5 %all-gather.7 = f32[64,64,16]{1,2,0:T(8,128)S(1)} all-gather(f32[1,64,16]{1,2,0:T(8,128)S(1)} %bitcast.71), channel_id=1, replica_groups=mesh['sep'=8,'row'=8,'col'=8] {'row','col'}, dimensions={0}, use_global_device_ids=true | all-gather | bytes 266240 | tf_op jit(solution)/shard_map/while/body/eval_jaxpr/all_gather | solution.py:53
  1368.7 1.9 collective-permute-start
  1370.6 9.7 collective-permute-done
  1380.6 48.0 %all-gather.6 = f32[64,64,16]{1,2,0:T(8,128)S(1)} all-gather(f32[1,64,16]{1,2,0:T(8,128)S(1)} %fusion.22), channel_id=1, replica_groups=mesh['sep'=8,'row'=8,'col'=8] {'row','col'}, dimensions={0}, use_global_device_ids=true | all-gather | bytes 266240 | tf_op jit(solution)/shard_map/while/body/eval_jaxpr/all_gather | solution.py:52
  1430.7 49.5 %all-gather.7 = f32[64,64,16]{1,2,0:T(8,128)S(1)} all-gather(f32[1,64,16]{1,2,0:T(8,128)S(1)} %bitcast.71), channel_id=1, replica_groups=mesh['sep'=8,'row'=8,'col'=8] {'row','col'}, dimensions={0}, use_global_device_ids=true | all-gather | bytes 266240 | tf_op jit(solution)/shard_map/while/body/eval_jaxpr/all_gather | solution.py:53
  1482.9 1.9 collective-permute-start
  1484.8 9.7 collective-permute-done
  1494.8 48.0 %all-gather.6 = f32[64,64,16]{1,2,0:T(8,128)S(1)} all-gather(f32[1,64,16]{1,2,0:T(8,128)S(1)} %fusion.22), channel_id=1, replica_groups=mesh['sep'=8,'row'=8,'col'=8] {'row','col'}, dimensions={0}, use_global_device_ids=true | all-gather | bytes 266240 | tf_op jit(solution)/shard_map/while/body/eval_jaxpr/all_gather | solution.py:52
  1544.9 49.5 %all-gather.7 = f32[64,64,16]{1,2,0:T(8,128)S(1)} all-gather(f32[1,64,16]{1,2,0:T(8,128)S(1)} %bitcast.71), channel_id=1, replica_groups=mesh['sep'=8,'row'=8,'col'=8] {'row','col'}, dimensions={0}, use_global_device_ids=true | all-gather | bytes 266240 | tf_op jit(solution)/shard_map/while/body/eval_jaxpr/all_gather | solution.py:53
  1597.1 1.9 collective-permute-start
  1599.0 9.7 collective-permute-done
  1609.0 48.0 %all-gather.6 = f32[64,64,16]{1,2,0:T(8,128)S(1)} all-gather(f32[1,64,16]{1,2,0:T(8,128)S(1)} %fusion.22), channel_id=1, replica_groups=mesh['sep'=8,'row'=8,'col'=8] {'row','col'}, dimensions={0}, use_global_device_ids=true | all-gather | bytes 266240 | tf_op jit(solution)/shard_map/while/body/eval_jaxpr/all_gather | solution.py:52
  1659.1 49.5 %all-gather.7 = f32[64,64,16]{1,2,0:T(8,128)S(1)} all-gather(f32[1,64,16]{1,2,0:T(8,128)S(1)} %bitcast.71), channel_id=1, replica_groups=mesh['sep'=8,'row'=8,'col'=8] {'row','col'}, dimensions={0}, use_global_device_ids=true | all-gather | bytes 266240 | tf_op jit(solution)/shard_map/while/body/eval_jaxpr/all_gather | solution.py:53
  1711.3 1.9 collective-permute-start
  1713.2 9.7 collective-permute-done
  1723.2 48.0 %all-gather.6 = f32[64,64,16]{1,2,0:T(8,128)S(1)} all-gather(f32[1,64,16]{1,2,0:T(8,128)S(1)} %fusion.22), channel_id=1, replica_groups=mesh['sep'=8,'row'=8,'col'=8] {'row','col'}, dimensions={0}, use_global_device_ids=true | all-gather | bytes 266240 | tf_op jit(solution)/shard_map/while/body/eval_jaxpr/all_gather | solution.py:52
  1773.3 49.5 %all-gather.7 = f32[64,64,16]{1,2,0:T(8,128)S(1)} all-gather(f32[1,64,16]{1,2,0:T(8,128)S(1)} %bitcast.71), channel_id=1, replica_groups=mesh['sep'=8,'row'=8,'col'=8] {'row','col'}, dimensions={0}, use_global_device_ids=true | all-gather | bytes 266240 | tf_op jit(solution)/shard_map/while/body/eval_jaxpr/all_gather | solution.py:53
  1827.4 9.7 collective-permute-done
  (298 shorter events, 83.6 us)
Async XLA Ops:
  0.0 0.7 copy-start.4
  0.7 0.7 copy-start.3
  58.1 1.2 copy-start
  109.9 1.0 copy-start.1
  112.5 11.7 collective-permute-start
  172.3 1.2 copy-start
  224.1 1.0 copy-start.1
  226.7 11.7 collective-permute-start
  286.5 1.2 copy-start
  338.3 1.0 copy-start.1
  340.9 11.7 collective-permute-start
  400.7 1.2 copy-start
  452.5 1.0 copy-start.1
  455.1 11.7 collective-permute-start
  514.9 1.2 copy-start
  566.7 1.0 copy-start.1
  569.3 11.7 collective-permute-start
  629.1 1.2 copy-start
  681.0 1.0 copy-start.1
  683.5 11.7 collective-permute-start
  743.3 1.2 copy-start
  795.2 1.0 copy-start.1
  797.7 11.7 collective-permute-start
  857.5 1.2 copy-start
  909.4 1.0 copy-start.1
  911.9 11.7 collective-permute-start
  971.7 1.2 copy-start
  1023.6 1.0 copy-start.1
  1026.1 11.7 collective-permute-start
  1085.9 1.2 copy-start
  1137.8 1.0 copy-start.1
  1140.3 11.7 collective-permute-start
  1200.1 1.2 copy-start
  1252.0 1.0 copy-start.1
  1254.5 11.7 collective-permute-start
  1314.3 1.2 copy-start
  1366.2 1.0 copy-start.1
  1368.7 11.7 collective-permute-start
  1428.5 1.2 copy-start
  1480.4 1.0 copy-start.1
  1482.9 11.7 collective-permute-start
  1542.7 1.2 copy-start
  1594.6 1.0 copy-start.1
  1597.1 11.7 collective-permute-start
  1657.0 1.2 copy-start
  1708.8 1.0 copy-start.1
  1711.3 11.7 collective-permute-start
  1771.2 1.2 copy-start
  1823.0 1.0 copy-start.1
  1825.5 11.7 collective-permute-start
  1837.2 0.6 copy-start.2
where the time goes:
time: 1840 us
  blocking collectives  1570 us (85%)
  waiting for transfers between devices  155 us (8%)
  local copies, waits for them, and re-layouts  33.2 us (2%)
  starting transfers between devices  31.4 us (2%)
  other arithmetic  25.5 us (1%)
  matrix products  23 us (1%)
    all_gather x16, blocking collectives, one_turn(): lax.all_gather(solved, ('row', 'col'), axis=1, tiled=True)  792 us
    all_gather x16, blocking collectives, one_turn(): lax.all_gather(resid, ('row', 'col'), axis=1, tiled=True)  776 us
    ppermute x16, waiting for transfers between devices, passed_along(): return lax.ppermute(block, axis, route)  155 us
  transfers between devices with their start and end apart: 16, of which 16 were waited for; matrix products, arithmetic and copies ran while one was open for 0% of the time, Pallas kernels for 0%

commit v1 on v0

--- a/solution.py
+++ b/solution.py
@@ -4,6 +4,14 @@
 from jax.sharding import PartitionSpec as P
 
 W = 4096
+
+
+def finish_table_in(my_data, shard_axis):
+    everything = jnp.stack([my_data] * jax.lax.axis_size(shard_axis))
+    right_arr = jnp.concatenate(
+        jax.lax.all_to_all(everything, axis_name=shard_axis, split_axis=0, concat_axis=0), axis=1
+    )
+    return right_arr
 
 
 def passed_along(block, axis, distance):
@@ -49,7 +57,7 @@
         batch_now = jnp.clip(batch_now, 0, batches - 1)
         given = lax.dynamic_index_in_dim(right_sides, batch_now, 0, keepdims=False)
         resid = given - lax.dynamic_slice_in_dim(carried, own_level * own_rows, own_rows, 1)
-        solved = solve_piece(lax.all_gather(resid, ("row", "col"), axis=1, tiled=True))
+        solved = solve_piece(finish_table_in(resid, ("row", "col")))
         update = lower_piece(lax.all_gather(solved, ("row", "col"), axis=1, tiled=True))
         update = jnp.where(live[None, :], update, jnp.float32(0.0))
         carried = carried.at[:, places].add(update)

time: 1840 us -> 1410 us (0.77)
  blocking collectives: 1570 us -> 783 us
  waiting for transfers between devices: 155 us -> 350 us
  starting transfers between devices: 31.4 us -> 137 us
  local copies, waits for them, and re-layouts: 33.2 us -> 72.1 us
    all_gather x16 -> x0, blocking collectives: 776 us -> none  [one_turn(): lax.all_gather(resid, ('row', 'col'), axis=1, tiled=True)]
    all_to_all x0 -> x16, waiting for transfers between devices: none -> 195 us  [finish_table_in(): jax.lax.all_to_all(everything, axis_name=shard_axis, split_axis=0, concat...]
    all_to_all x0 -> x16, starting transfers between devices: none -> 105 us  [finish_table_in(): jax.lax.all_to_all(everything, axis_name=shard_axis, split_axis=0, concat...]
    while x128, local copies, waits for them, and re-layouts: 24.4 us -> 49.1 us
    all_to_all x0 -> x16, other arithmetic: none -> 18.7 us  [finish_table_in(): jax.lax.all_to_all(everything, axis_name=shard_axis, split_axis=0, concat...]
  transfers between devices with their start and end apart: 16 -> 32, of which waited for: 16 -> 32; matrix products, arithmetic and copies ran while one was open for 0% -> 1% of each run, Pallas kernels for 0% -> 0%
where the time goes in v1:
time: 1410 us
  blocking collectives  783 us (56%)
  waiting for transfers between devices  350 us (25%)
  starting transfers between devices  137 us (10%)
  local copies, waits for them, and re-layouts  72.1 us (5%)
  other arithmetic  43.2 us (3%)
  matrix products  23 us (2%)
    all_gather x16, blocking collectives, one_turn(): lax.all_gather(solved, ('row', 'col'), axis=1, tiled=True)  783 us
    all_to_all x16, waiting for transfers between devices, finish_table_in(): jax.lax.all_to_all(everything, axis_name=shard_axis, split_axis=0, concat...  195 us
    ppermute x16, waiting for transfers between devices, passed_along(): return lax.ppermute(block, axis, route)  155 us
    all_to_all x16, starting transfers between devices, finish_table_in(): jax.lax.all_to_all(everything, axis_name=shard_axis, split_axis=0, concat...  105 us
    while x128, local copies, waits for them, and re-layouts  49.1 us
    ppermute x16, starting transfers between devices, passed_along(): return lax.ppermute(block, axis, route)  31.4 us
  transfers between devices with their start and end apart: 32, of which 32 were waited for; matrix products, arithmetic and copies ran while one was open for 1% of the time, Pallas kernels for 0%

profile of v1, /device:TPU:32, one launch (start us, length us, event | category | flops | bytes accessed | tf_op | source)
XLA Modules:
  0.0 1410.6 jit_solution(3811199146350053031)
XLA Ops:
  1.4 1408.6 %while.18 = (s32[]{:T(128)}, f32[16,512]{0,1:T(8,128)S(1)}, f32[2,16,64]{2,1,0:T(8,128)S(1)}, s32[32]{0:T(128)S(1)}, f32[2,16,64]{2,1,0:T(8,128)S(1)}, /*index=5...) while((s32[]{:T(128)}, f32[16,512]{0,1:T(8,128)S(1)}, ...), condition=%wide.region_2.3_spmd.clone, body=%wide.region_0.2_spmd.clone.sunk | while | flops 75500688 | bytes 13656974 | solution.py:74
  2.7 13.8 all-to-all-start
  17.1 12.2 all-to-all-done
  33.3 48.9 %all-gather.3 = f32[64,64,16]{1,2,0:T(8,128)S(1)} all-gather(f32[1,64,16]{1,2,0:T(8,128)S(1)} %bitcast.65), channel_id=1, replica_groups=mesh['sep'=8,'row'=8,'col'=8] {'row','col'}, dimensions={0}, use_global_device_ids=true | all-gather | bytes 266240 | tf_op jit(solution)/shard_map/while/body/eval_jaxpr/all_gather | solution.py:61
  87.5 9.1 collective-permute-done
  97.9 6.1 all-to-all-start
  104.7 12.2 all-to-all-done
  120.9 48.9 %all-gather.3 = f32[64,64,16]{1,2,0:T(8,128)S(1)} all-gather(f32[1,64,16]{1,2,0:T(8,128)S(1)} %bitcast.65), channel_id=1, replica_groups=mesh['sep'=8,'row'=8,'col'=8] {'row','col'}, dimensions={0}, use_global_device_ids=true | all-gather | bytes 266240 | tf_op jit(solution)/shard_map/while/body/eval_jaxpr/all_gather | solution.py:61
  174.4 9.7 collective-permute-done
  185.5 6.1 all-to-all-start
  192.2 12.2 all-to-all-done
  208.4 48.9 %all-gather.3 = f32[64,64,16]{1,2,0:T(8,128)S(1)} all-gather(f32[1,64,16]{1,2,0:T(8,128)S(1)} %bitcast.65), channel_id=1, replica_groups=mesh['sep'=8,'row'=8,'col'=8] {'row','col'}, dimensions={0}, use_global_device_ids=true | all-gather | bytes 266240 | tf_op jit(solution)/shard_map/while/body/eval_jaxpr/all_gather | solution.py:61
  262.0 9.7 collective-permute-done
  273.0 6.1 all-to-all-start
  279.8 12.2 all-to-all-done
  296.0 48.9 %all-gather.3 = f32[64,64,16]{1,2,0:T(8,128)S(1)} all-gather(f32[1,64,16]{1,2,0:T(8,128)S(1)} %bitcast.65), channel_id=1, replica_groups=mesh['sep'=8,'row'=8,'col'=8] {'row','col'}, dimensions={0}, use_global_device_ids=true | all-gather | bytes 266240 | tf_op jit(solution)/shard_map/while/body/eval_jaxpr/all_gather | solution.py:61
  349.5 9.7 collective-permute-done
  360.6 6.1 all-to-all-start
  367.4 12.2 all-to-all-done
  383.5 48.9 %all-gather.3 = f32[64,64,16]{1,2,0:T(8,128)S(1)} all-gather(f32[1,64,16]{1,2,0:T(8,128)S(1)} %bitcast.65), channel_id=1, replica_groups=mesh['sep'=8,'row'=8,'col'=8] {'row','col'}, dimensions={0}, use_global_device_ids=true | all-gather | bytes 266240 | tf_op jit(solution)/shard_map/while/body/eval_jaxpr/all_gather | solution.py:61
  437.1 9.7 collective-permute-done
  448.1 6.1 all-to-all-start
  454.9 12.2 all-to-all-done
  471.1 48.9 %all-gather.3 = f32[64,64,16]{1,2,0:T(8,128)S(1)} all-gather(f32[1,64,16]{1,2,0:T(8,128)S(1)} %bitcast.65), channel_id=1, replica_groups=mesh['sep'=8,'row'=8,'col'=8] {'row','col'}, dimensions={0}, use_global_device_ids=true | all-gather | bytes 266240 | tf_op jit(solution)/shard_map/while/body/eval_jaxpr/all_gather | solution.py:61
  524.7 9.7 collective-permute-done
  535.7 6.1 all-to-all-start
  542.5 12.2 all-to-all-done
  558.7 48.9 %all-gather.3 = f32[64,64,16]{1,2,0:T(8,128)S(1)} all-gather(f32[1,64,16]{1,2,0:T(8,128)S(1)} %bitcast.65), channel_id=1, replica_groups=mesh['sep'=8,'row'=8,'col'=8] {'row','col'}, dimensions={0}, use_global_device_ids=true | all-gather | bytes 266240 | tf_op jit(solution)/shard_map/while/body/eval_jaxpr/all_gather | solution.py:61
  612.2 9.7 collective-permute-done
  623.3 6.1 all-to-all-start
  630.0 12.2 all-to-all-done
  646.2 48.9 %all-gather.3 = f32[64,64,16]{1,2,0:T(8,128)S(1)} all-gather(f32[1,64,16]{1,2,0:T(8,128)S(1)} %bitcast.65), channel_id=1, replica_groups=mesh['sep'=8,'row'=8,'col'=8] {'row','col'}, dimensions={0}, use_global_device_ids=true | all-gather | bytes 266240 | tf_op jit(solution)/shard_map/while/body/eval_jaxpr/all_gather | solution.py:61
  699.8 9.7 collective-permute-done
  710.8 6.1 all-to-all-start
  717.6 12.2 all-to-all-done
  733.8 48.9 %all-gather.3 = f32[64,64,16]{1,2,0:T(8,128)S(1)} all-gather(f32[1,64,16]{1,2,0:T(8,128)S(1)} %bitcast.65), channel_id=1, replica_groups=mesh['sep'=8,'row'=8,'col'=8] {'row','col'}, dimensions={0}, use_global_device_ids=true | all-gather | bytes 266240 | tf_op jit(solution)/shard_map/while/body/eval_jaxpr/all_gather | solution.py:61
  787.3 9.7 collective-permute-done
  798.4 6.1 all-to-all-start
  805.2 12.2 all-to-all-done
  821.3 48.9 %all-gather.3 = f32[64,64,16]{1,2,0:T(8,128)S(1)} all-gather(f32[1,64,16]{1,2,0:T(8,128)S(1)} %bitcast.65), channel_id=1, replica_groups=mesh['sep'=8,'row'=8,'col'=8] {'row','col'}, dimensions={0}, use_global_device_ids=true | all-gather | bytes 266240 | tf_op jit(solution)/shard_map/while/body/eval_jaxpr/all_gather | solution.py:61
  874.9 9.7 collective-permute-done
  885.9 6.1 all-to-all-start
  892.7 12.2 all-to-all-done
  908.9 48.9 %all-gather.3 = f32[64,64,16]{1,2,0:T(8,128)S(1)} all-gather(f32[1,64,16]{1,2,0:T(8,128)S(1)} %bitcast.65), channel_id=1, replica_groups=mesh['sep'=8,'row'=8,'col'=8] {'row','col'}, dimensions={0}, use_global_device_ids=true | all-gather | bytes 266240 | tf_op jit(solution)/shard_map/while/body/eval_jaxpr/all_gather | solution.py:61
  962.4 9.7 collective-permute-done
  973.5 6.1 all-to-all-start
  980.3 12.2 all-to-all-done
  996.5 48.9 %all-gather.3 = f32[64,64,16]{1,2,0:T(8,128)S(1)} all-gather(f32[1,64,16]{1,2,0:T(8,128)S(1)} %bitcast.65), channel_id=1, replica_groups=mesh['sep'=8,'row'=8,'col'=8] {'row','col'}, dimensions={0}, use_global_device_ids=true | all-gather | bytes 266240 | tf_op jit(solution)/shard_map/while/body/eval_jaxpr/all_gather | solution.py:61
  1050.0 9.7 collective-permute-done
  1061.0 6.1 all-to-all-start
  1067.8 12.2 all-to-all-done
  1084.0 48.9 %all-gather.3 = f32[64,64,16]{1,2,0:T(8,128)S(1)} all-gather(f32[1,64,16]{1,2,0:T(8,128)S(1)} %bitcast.65), channel_id=1, replica_groups=mesh['sep'=8,'row'=8,'col'=8] {'row','col'}, dimensions={0}, use_global_device_ids=true | all-gather | bytes 266240 | tf_op jit(solution)/shard_map/while/body/eval_jaxpr/all_gather | solution.py:61
  1137.6 9.7 collective-permute-done
  1148.6 6.1 all-to-all-start
  1155.4 12.2 all-to-all-done
  1171.6 48.9 %all-gather.3 = f32[64,64,16]{1,2,0:T(8,128)S(1)} all-gather(f32[1,64,16]{1,2,0:T(8,128)S(1)} %bitcast.65), channel_id=1, replica_groups=mesh['sep'=8,'row'=8,'col'=8] {'row','col'}, dimensions={0}, use_global_device_ids=true | all-gather | bytes 266240 | tf_op jit(solution)/shard_map/while/body/eval_jaxpr/all_gather | solution.py:61
  1225.1 9.7 collective-permute-done
  1236.2 6.1 all-to-all-start
  1243.0 12.2 all-to-all-done
  1259.1 48.9 %all-gather.3 = f32[64,64,16]{1,2,0:T(8,128)S(1)} all-gather(f32[1,64,16]{1,2,0:T(8,128)S(1)} %bitcast.65), channel_id=1, replica_groups=mesh['sep'=8,'row'=8,'col'=8] {'row','col'}, dimensions={0}, use_global_device_ids=true | all-gather | bytes 266240 | tf_op jit(solution)/shard_map/while/body/eval_jaxpr/all_gather | solution.py:61
  1312.7 9.7 collective-permute-done
  1330.5 12.2 all-to-all-done
  1346.7 48.9 %all-gather.3 = f32[64,64,16]{1,2,0:T(8,128)S(1)} all-gather(f32[1,64,16]{1,2,0:T(8,128)S(1)} %bitcast.65), channel_id=1, replica_groups=mesh['sep'=8,'row'=8,'col'=8] {'row','col'}, dimensions={0}, use_global_device_ids=true | all-gather | bytes 266240 | tf_op jit(solution)/shard_map/while/body/eval_jaxpr/all_gather | solution.py:61
  1400.2 9.7 collective-permute-done
  (410 shorter events, 175.8 us)
Async XLA Ops:
  2.7 26.7 %all-to-all-start = ((f32[64,1,1024]{2,1,0:T(1,128)}), f32[64,1,1024]{2,1,0:T(1,128)S(1)}, u32[]{:S(2)}, u32[]{:S(2)}) async-start(f32[64,1,1024]{2,1,0:T(1,128)} %reshape.71), calls=%async_computation | async-start | bytes 524288 | tf_op jit(solution)/shard_map/while/body/eval_jaxpr/all_to_all | solution.py:12
  31.2 1.2 copy-start
  82.4 1.0 copy-start.1
  84.9 11.7 collective-permute-start
  97.9 19.0 %all-to-all-start = ((f32[64,1,1024]{2,1,0:T(1,128)}), f32[64,1,1024]{2,1,0:T(1,128)S(1)}, u32[]{:S(2)}, u32[]{:S(2)}) async-start(f32[64,1,1024]{2,1,0:T(1,128)} %reshape.71), calls=%async_computation | async-start | bytes 524288 | tf_op jit(solution)/shard_map/while/body/eval_jaxpr/all_to_all | solution.py:12
  118.7 1.2 copy-start
  170.0 1.0 copy-start.1
  172.5 11.7 collective-permute-start
  185.5 19.0 %all-to-all-start = ((f32[64,1,1024]{2,1,0:T(1,128)}), f32[64,1,1024]{2,1,0:T(1,128)S(1)}, u32[]{:S(2)}, u32[]{:S(2)}) async-start(f32[64,1,1024]{2,1,0:T(1,128)} %reshape.71), calls=%async_computation | async-start | bytes 524288 | tf_op jit(solution)/shard_map/while/body/eval_jaxpr/all_to_all | solution.py:12
  206.3 1.2 copy-start
  257.5 1.0 copy-start.1
  260.0 11.7 collective-permute-start
  273.0 19.0 %all-to-all-start = ((f32[64,1,1024]{2,1,0:T(1,128)}), f32[64,1,1024]{2,1,0:T(1,128)S(1)}, u32[]{:S(2)}, u32[]{:S(2)}) async-start(f32[64,1,1024]{2,1,0:T(1,128)} %reshape.71), calls=%async_computation | async-start | bytes 524288 | tf_op jit(solution)/shard_map/while/body/eval_jaxpr/all_to_all | solution.py:12
  293.8 1.2 copy-start
  345.1 1.0 copy-start.1
  347.6 11.7 collective-permute-start
  360.6 19.0 %all-to-all-start = ((f32[64,1,1024]{2,1,0:T(1,128)}), f32[64,1,1024]{2,1,0:T(1,128)S(1)}, u32[]{:S(2)}, u32[]{:S(2)}) async-start(f32[64,1,1024]{2,1,0:T(1,128)} %reshape.71), calls=%async_computation | async-start | bytes 524288 | tf_op jit(solution)/shard_map/while/body/eval_jaxpr/all_to_all | solution.py:12
  381.4 1.2 copy-start
  432.6 1.0 copy-start.1
  435.2 11.7 collective-permute-start
  448.1 19.0 %all-to-all-start = ((f32[64,1,1024]{2,1,0:T(1,128)}), f32[64,1,1024]{2,1,0:T(1,128)S(1)}, u32[]{:S(2)}, u32[]{:S(2)}) async-start(f32[64,1,1024]{2,1,0:T(1,128)} %reshape.71), calls=%async_computation | async-start | bytes 524288 | tf_op jit(solution)/shard_map/while/body/eval_jaxpr/all_to_all | solution.py:12
  469.0 1.2 copy-start
  520.2 1.0 copy-start.1
  522.7 11.7 collective-permute-start
  535.7 19.0 %all-to-all-start = ((f32[64,1,1024]{2,1,0:T(1,128)}), f32[64,1,1024]{2,1,0:T(1,128)S(1)}, u32[]{:S(2)}, u32[]{:S(2)}) async-start(f32[64,1,1024]{2,1,0:T(1,128)} %reshape.71), calls=%async_computation | async-start | bytes 524288 | tf_op jit(solution)/shard_map/while/body/eval_jaxpr/all_to_all | solution.py:12
  556.5 1.2 copy-start
  607.8 1.0 copy-start.1
  610.3 11.7 collective-permute-start
  623.3 19.0 %all-to-all-start = ((f32[64,1,1024]{2,1,0:T(1,128)}), f32[64,1,1024]{2,1,0:T(1,128)S(1)}, u32[]{:S(2)}, u32[]{:S(2)}) async-start(f32[64,1,1024]{2,1,0:T(1,128)} %reshape.71), calls=%async_computation | async-start | bytes 524288 | tf_op jit(solution)/shard_map/while/body/eval_jaxpr/all_to_all | solution.py:12
  644.1 1.2 copy-start
  695.3 1.0 copy-start.1
  697.8 11.7 collective-permute-start
  710.8 19.0 %all-to-all-start = ((f32[64,1,1024]{2,1,0:T(1,128)}), f32[64,1,1024]{2,1,0:T(1,128)S(1)}, u32[]{:S(2)}, u32[]{:S(2)}) async-start(f32[64,1,1024]{2,1,0:T(1,128)} %reshape.71), calls=%async_computation | async-start | bytes 524288 | tf_op jit(solution)/shard_map/while/body/eval_jaxpr/all_to_all | solution.py:12
  731.6 1.2 copy-start
  782.9 1.0 copy-start.1
  785.4 11.7 collective-permute-start
  798.4 19.0 %all-to-all-start = ((f32[64,1,1024]{2,1,0:T(1,128)}), f32[64,1,1024]{2,1,0:T(1,128)S(1)}, u32[]{:S(2)}, u32[]{:S(2)}) async-start(f32[64,1,1024]{2,1,0:T(1,128)} %reshape.71), calls=%async_computation | async-start | bytes 524288 | tf_op jit(solution)/shard_map/while/body/eval_jaxpr/all_to_all | solution.py:12
  819.2 1.2 copy-start
  870.4 1.0 copy-start.1
  873.0 11.7 collective-permute-start
  885.9 19.0 %all-to-all-start = ((f32[64,1,1024]{2,1,0:T(1,128)}), f32[64,1,1024]{2,1,0:T(1,128)S(1)}, u32[]{:S(2)}, u32[]{:S(2)}) async-start(f32[64,1,1024]{2,1,0:T(1,128)} %reshape.71), calls=%async_computation | async-start | bytes 524288 | tf_op jit(solution)/shard_map/while/body/eval_jaxpr/all_to_all | solution.py:12
  906.7 1.2 copy-start
  958.0 1.0 copy-start.1
  960.5 11.7 collective-permute-start
  973.5 19.0 %all-to-all-start = ((f32[64,1,1024]{2,1,0:T(1,128)}), f32[64,1,1024]{2,1,0:T(1,128)S(1)}, u32[]{:S(2)}, u32[]{:S(2)}) async-start(f32[64,1,1024]{2,1,0:T(1,128)} %reshape.71), calls=%async_computation | async-start | bytes 524288 | tf_op jit(solution)/shard_map/while/body/eval_jaxpr/all_to_all | solution.py:12
  994.3 1.2 copy-start
  1045.6 1.0 copy-start.1
  1048.1 11.7 collective-permute-start
  1061.0 19.0 %all-to-all-start = ((f32[64,1,1024]{2,1,0:T(1,128)}), f32[64,1,1024]{2,1,0:T(1,128)S(1)}, u32[]{:S(2)}, u32[]{:S(2)}) async-start(f32[64,1,1024]{2,1,0:T(1,128)} %reshape.71), calls=%async_computation | async-start | bytes 524288 | tf_op jit(solution)/shard_map/while/body/eval_jaxpr/all_to_all | solution.py:12
  1081.9 1.2 copy-start
  1133.1 1.0 copy-start.1
  1135.6 11.7 collective-permute-start
  1148.6 19.0 %all-to-all-start = ((f32[64,1,1024]{2,1,0:T(1,128)}), f32[64,1,1024]{2,1,0:T(1,128)S(1)}, u32[]{:S(2)}, u32[]{:S(2)}) async-start(f32[64,1,1024]{2,1,0:T(1,128)} %reshape.71), calls=%async_computation | async-start | bytes 524288 | tf_op jit(solution)/shard_map/while/body/eval_jaxpr/all_to_all | solution.py:12
  1169.4 1.2 copy-start
  1220.7 1.0 copy-start.1
  1223.2 11.7 collective-permute-start
  1236.2 19.0 %all-to-all-start = ((f32[64,1,1024]{2,1,0:T(1,128)}), f32[64,1,1024]{2,1,0:T(1,128)S(1)}, u32[]{:S(2)}, u32[]{:S(2)}) async-start(f32[64,1,1024]{2,1,0:T(1,128)} %reshape.71), calls=%async_computation | async-start | bytes 524288 | tf_op jit(solution)/shard_map/while/body/eval_jaxpr/all_to_all | solution.py:12
  1257.0 1.2 copy-start
  1308.2 1.0 copy-start.1
  1310.8 11.7 collective-permute-start
  1323.7 19.0 %all-to-all-start = ((f32[64,1,1024]{2,1,0:T(1,128)}), f32[64,1,1024]{2,1,0:T(1,128)S(1)}, u32[]{:S(2)}, u32[]{:S(2)}) async-start(f32[64,1,1024]{2,1,0:T(1,128)} %reshape.71), calls=%async_computation | async-start | bytes 524288 | tf_op jit(solution)/shard_map/while/body/eval_jaxpr/all_to_all | solution.py:12
  1344.5 1.2 copy-start
  1395.8 1.0 copy-start.1
  1398.3 11.7 collective-permute-start
  (3 other events, 2.0 us)
